TPU v7x, 32 devices: a whole 2x2x4 slice. The times are simulated.
32 devices in a mesh: rep: 2 (over y), grp: 4 (over z), sub: 4 (over x, core).
Axes of the slice: x: 2, y: 2, z: 4, core: 2. Of those that a mesh axis runs over, the one named last changes fastest.
Arguments:
- volume: bfloat16 [256, 8, 8, 128], P(None, ('rep', 'grp'), 'sub'), parts along dimension 1, may hold values from -6 to 6
- cotangent: bfloat16 [256, 8, 8, 128], P(None, ('rep', 'grp'), 'sub'), parts along dimension 1, may hold values from -6 to 6
- first_weight: bfloat16 [256, 256], replicated, may hold values from -0.375 to 0.375
- group_weight: bfloat16 [256, 8, 3, 3, 3], replicated, may hold values from -0.4375 to 0.4375
- third_weight: bfloat16 [256, 256], replicated, may hold values from -0.375 to 0.375
Outputs:
- block_output: bfloat16 [256, 8, 8, 128], P(None, ('rep', 'grp'), 'sub'), parts along dimension 1
- volume_grad: bfloat16 [256, 8, 8, 128], P(None, ('rep', 'grp'), 'sub'), parts along dimension 1
- first_grad: float32 [512, 256], P('rep'), parts along dimension 0
- group_grad: float32 [512, 8, 3, 3, 3], P(('rep', 'grp')), parts along dimension 0
- third_grad: float32 [512, 256], P('rep'), parts along dimension 0
There are 2 independent parts, one for each index of `rep`. A program takes and returns all parts, laid end to end along the dimension named above; an argument that names none is the same for every part. Nothing has to cross between parts.
All inputs are finite; a program needn't handle non-finite values.
Results may differ from a plain program's by a relative error of at most 0.0073.
Values may be sent and summed in bfloat16 or wider, within the bound.
No kernel may reach another device: no remote copies, remote signals or barrier semaphores. Data moves between devices by JAX's collectives and lax.ppermute only.
A program may use at most 64 MiB of HBM per device.

v0:
```python
import math
import jax
import jax.numpy as jnp
from jax import lax
from jax.sharding import PartitionSpec as P

GW = 8


def padded_2(block, sides, width):
    for axis, dim in sides:
        count = lax.axis_size(axis)
        forward = [(i, i + 1) for i in range(count - 1)]
        backward = [(target, source) for source, target in forward]
        low = lax.ppermute(
            lax.slice_in_dim(block, block.shape[dim] - width, None, axis=dim), axis, forward
        )
        high = lax.ppermute(lax.slice_in_dim(block, 0, width, axis=dim), axis, backward)
        block = jnp.concatenate([low, block, high], axis=dim)
    return block


def silu_slope(values):
    sigma = jax.nn.sigmoid(values)
    return sigma * (1.0 + values * (1.0 - sigma))


def dense_conv(source, kernel, depth_pad):
    padding = ((depth_pad, depth_pad), (0, 0), (1, 1))
    return lax.conv_general_dilated(
        source[None],
        kernel,
        (1, 1, 1),
        padding,
        dimension_numbers=("NCDHW", "OIDHW", "NCDHW"),
        preferred_element_type=jnp.float32,
    )[0]


def block_diagonal(kernel):
    rows = kernel.shape[0]
    tiled = jnp.tile(kernel, (1, rows // GW, 1, 1, 1))
    group_of = jnp.arange(rows) // GW
    mask = (group_of[:, None] == group_of[None, :]).astype(kernel.dtype)
    return tiled * mask[:, :, None, None, None]


def diagonal_blocks(dense):
    rows = dense.shape[1]
    groups = rows // GW
    shaped = dense.reshape(groups, GW, rows, *dense.shape[2:])
    group_of = jnp.arange(rows) // GW
    mask = (jnp.arange(groups)[:, None] == group_of[None, :]).astype(dense.dtype)
    picked = (shaped * mask[:, None, :, None, None, None]).sum(axis=0)
    return picked.transpose(1, 0, 2, 3, 4)


def weight_grad(padded, deltas):
    return lax.conv_general_dilated(
        padded[None],
        deltas[None],
        (1, 1, 1),
        "VALID",
        dimension_numbers=("CNDHW", "IODHW", "NCDHW"),
        preferred_element_type=jnp.float32,
    )


def per_device(volume, cotangent, first_weight, group_weight, third_weight):
    channels, depth, height, width = volume.shape
    flattened = volume.reshape(channels, -1)
    contract_lead = (((0,), (0,)), ((), ()))
    contract_tail = (((1,), (1,)), ((), ()))
    total_cells = depth * lax.axis_size("grp") * height * lax.axis_size("sub") * width
    factor = 1.0 / math.sqrt(total_cells)
    group_rows = channels // lax.axis_size("grp")
    first_pre = lax.dot_general(
        first_weight, flattened, contract_lead, preferred_element_type=jnp.float32
    )
    first_act = jax.nn.silu(first_pre).astype(jnp.bfloat16).reshape(volume.shape)
    own_kernel = lax.dynamic_slice_in_dim(
        group_weight, lax.axis_index("grp") * group_rows, group_rows, 0
    )
    dense_kernel = block_diagonal(own_kernel)
    gathered = lax.all_to_all(first_act, "grp", split_axis=0, concat_axis=1, tiled=True)
    padded_act = padded_2(gathered, (("sub", 2),), 1)
    group_pre = dense_conv(padded_act, dense_kernel, 1)
    group_act = jax.nn.silu(group_pre).astype(jnp.bfloat16)
    returned = lax.all_to_all(group_act, "grp", split_axis=1, concat_axis=0, tiled=True)
    act_flat = returned.reshape(channels, -1)
    summed = flattened.astype(jnp.float32) + lax.dot_general(
        third_weight, act_flat, contract_lead, preferred_element_type=jnp.float32
    )
    block_output = jax.nn.silu(summed).astype(jnp.bfloat16).reshape(volume.shape)
    third_delta = (cotangent.reshape(channels, -1).astype(jnp.float32) * silu_slope(summed)).astype(
        jnp.bfloat16
    )
    third_part = lax.dot_general(
        act_flat, third_delta, contract_tail, preferred_element_type=jnp.float32
    )
    third_grad = lax.psum(third_part, ("grp", "sub")) * factor
    hidden_grad = (
        jnp.dot(third_weight, third_delta, preferred_element_type=jnp.float32)
        .astype(jnp.bfloat16)
        .reshape(volume.shape)
    )
    arriving = lax.all_to_all(hidden_grad, "grp", split_axis=0, concat_axis=1, tiled=True)
    group_delta = (arriving.astype(jnp.float32) * silu_slope(group_pre)).astype(jnp.bfloat16)
    delta_rim = padded_2(group_delta, (("sub", 2),), 1)
    flipped = dense_kernel.transpose(1, 0, 2, 3, 4)[:, :, ::-1, ::-1, ::-1]
    inner_local = dense_conv(delta_rim, flipped, 1).astype(jnp.bfloat16)
    dense_grad = weight_grad(jnp.pad(padded_act, ((0, 0), (1, 1), (0, 0), (1, 1))), group_delta)
    kernel_part = diagonal_blocks(dense_grad)
    inner_grad = lax.all_to_all(inner_local, "grp", split_axis=1, concat_axis=0, tiled=True)
    group_grad = lax.psum(kernel_part, "sub") * factor
    first_delta = (
        inner_grad.reshape(channels, -1).astype(jnp.float32) * silu_slope(first_pre)
    ).astype(jnp.bfloat16)
    first_part = lax.dot_general(
        flattened, first_delta, contract_tail, preferred_element_type=jnp.float32
    )
    volume_grad = (
        (
            third_delta.astype(jnp.float32)
            + jnp.dot(first_weight, first_delta, preferred_element_type=jnp.float32)
        )
        .astype(jnp.bfloat16)
        .reshape(volume.shape)
    )
    first_grad = lax.psum(first_part, ("grp", "sub")) * factor
    return (block_output, volume_grad, first_grad, group_grad, third_grad)


def solution(mesh):
    in_specs = (
        P(None, ("rep", "grp"), "sub", None),
        P(None, ("rep", "grp"), "sub", None),
        P(),
        P(),
        P(),
    )
    out_specs = (
        P(None, ("rep", "grp"), "sub", None),
        P(None, ("rep", "grp"), "sub", None),
        P("rep", None),
        P(("rep", "grp"), None, None, None, None),
        P("rep", None),
    )
    return jax.shard_map(
        per_device, mesh=mesh, in_specs=in_specs, out_specs=out_specs, check_vma=False
    )
```

profile of v0, /device:TPU:1, one launch (start us, length us, event | category | flops | bytes accessed | tf_op | source)
XLA Modules:
  0.0 194.1 jit_solution(14904769792690059259)
XLA Ops:
  7.2 0.0 copy-start
  7.2 1.0 copy.70
  8.2 0.0 copy-start.4
  8.2 1.8 multiply_convert_fusion.2
  10.1 0.8 copy.71
  10.9 5.4 %all-to-all-start = ((bf16[256,1,2,128]{3,2,1,0:T(2,128)(2,1)}), bf16[256,1,2,128]{3,2,1,0:T(2,128)(2,1)S(1)}, u32[]{:S(2)}, u32[]{:S(2)}) async-start(bf16[256,1,2,128]{3,2,1,0:T(2,128)(2,1)} %copy.71), calls=%async_computation | async-start | bytes 262144 | tf_op jit(solution)/shard_map/all_to_all | solution.py:85
  16.3 0.1 compare_convert_fusion
  16.4 4.7 %all-to-all-done = bf16[256,1,2,128]{3,2,1,0:T(2,128)(2,1)S(1)} async-done(((bf16[256,1,2,128]{3,2,1,0:T(2,128)(2,1)}), bf16[256,1,2,128]{3,2,1,0:T(2,128)(2,1)S(1)}, u32[]{:S(2)}, u32[]{:S(2)}) %all-to-all-start) | async-done | bytes 131104 | tf_op jit(solution)/shard_map/all_to_all | solution.py:85
  21.1 5.2 %collective-permute-start = (bf16[64,4,1,128]{3,0,1,2:T(8,128)(2,1)S(1)}, bf16[64,4,1,128]{3,0,1,2:T(8,128)(2,1)S(1)}, u32[]{:S(2)}, u32[]{:S(2)}) collective-permute-start(bf16[64,4,1,128]{3,0,1,2:T(8,128)(2,1)S(1)} %get-tuple-element.33), channel_id=1, source_target_pairs={{0,1},{1,2},{2,3},{4,5},{5,6},{6,7},{8,9},{9,10},{10,11},{12,13},{... | collective-permute-start | bytes 196616 | tf_op jit(solution)/shard_map/ppermute | solution.py:15
  26.4 1.9 collective-permute-start.1
  28.3 0.1 constant_dynamic-slice_fusion
  28.4 3.5 %collective-permute-done.1 = bf16[64,4,1,128]{3,0,1,2:T(8,128)(2,1)S(1)} collective-permute-done((bf16[64,4,1,128]{3,0,1,2:T(8,128)(2,1)S(1)}, bf16[64,4,1,128]{3,0,1,2:T(8,128)(2,1)S(1)}, u32[]{:S(2)}, u32[]{:S(2)}) %collective-permute-start.1) | collective-permute-done | bytes 65568 | tf_op jit(solution)/shard_map/ppermute | solution.py:18
  32.0 0.3 copy.107
  32.3 0.0 copy-start.5
  32.3 0.3 pad.5.clone
  32.6 0.1 copy.75
  32.7 0.3 copy-done.5
  33.0 1.2 add_multiply_fusion
  34.2 0.3 copy.76
  34.6 0.2 copy.105
  34.8 0.7 fusion.28
  35.5 3.3 %all-to-all-start.1 = ((bf16[64,4,2,128]{3,0,2,1:T(8,128)(2,1)}), bf16[64,4,2,128]{3,0,2,1:T(8,128)(2,1)S(1)}, u32[]{:S(2)}, u32[]{:S(2)}) async-start(bf16[64,4,2,128]{3,0,2,1:T(8,128)(2,1)} %fusion.28), calls=%async_computation.1 | async-start | bytes 262144 | tf_op jit(solution)/shard_map/all_to_all | solution.py:89
  38.9 0.8 copy.79
  39.7 0.3 copy.91
  40.0 0.2 copy.106
  40.2 0.2 pad_bitcast_fusion
  40.5 1.7 copy.93
  42.2 1.4 all-to-all-done.1
  43.6 0.1 copy.78
  43.7 1.3 fusion.24
  45.0 0.2 convolution_convert_fusion
  45.2 0.8 copy.80
  46.0 3.3 %all-to-all-start.2 = ((bf16[256,1,2,128]{3,2,1,0:T(2,128)(2,1)}), bf16[256,1,2,128]{3,2,1,0:T(2,128)(2,1)S(1)}, u32[]{:S(2)}, u32[]{:S(2)}) async-start(bf16[256,1,2,128]{3,2,1,0:T(2,128)(2,1)} %copy.80), calls=%async_computation.2 | async-start | bytes 262144 | tf_op jit(solution)/shard_map/all_to_all | solution.py:107
  49.4 0.8 copy.96
  50.1 0.9 fusion.35
  51.1 3.5 %all-to-all-done.2 = bf16[256,1,2,128]{3,2,1,0:T(2,128)(2,1)S(1)} async-done(((bf16[256,1,2,128]{3,2,1,0:T(2,128)(2,1)}), bf16[256,1,2,128]{3,2,1,0:T(2,128)(2,1)S(1)}, u32[]{:S(2)}, u32[]{:S(2)}) %all-to-all-start.2) | async-done | bytes 131104 | tf_op jit(solution)/shard_map/all_to_all | solution.py:107
  54.6 0.1 fusion.23
  54.8 3.7 %collective-permute-start.2 = (bf16[64,4,1,128]{3,0,2,1:T(8,128)(2,1)S(1)}, bf16[64,4,1,128]{3,0,2,1:T(8,128)(2,1)S(1)}, u32[]{:S(2)}, u32[]{:S(2)}) collective-permute-start(bf16[64,4,1,128]{3,0,2,1:T(8,128)(2,1)S(1)} %get-tuple-element.31), channel_id=1, source_target_pairs={{0,1},{1,2},{2,3},{4,5},{5,6},{6,7},{8,9},{9,10},{10,11},{12,13},{... | collective-permute-start | bytes 196616 | tf_op jit(solution)/shard_map/ppermute | solution.py:15
  58.4 1.9 collective-permute-start.3
  60.4 0.4 copy.94
  60.8 3.2 %collective-permute-done.3 = bf16[64,4,1,128]{3,0,2,1:T(8,128)(2,1)S(1)} collective-permute-done((bf16[64,4,1,128]{3,0,2,1:T(8,128)(2,1)S(1)}, bf16[64,4,1,128]{3,0,2,1:T(8,128)(2,1)S(1)}, u32[]{:S(2)}, u32[]{:S(2)}) %collective-permute-start.3) | collective-permute-done | bytes 65568 | tf_op jit(solution)/shard_map/ppermute | solution.py:18
  64.1 0.3 copy.108
  64.4 0.3 pad.7.clone
  64.7 0.1 copy.85
  64.8 2.1 %fusion.4 = bf16[4,2,8,17,64]{4,2,3,1,0:T(8,128)(2,1)S(1)} fusion(bf16[64,4,4,1,7,2]{0,4,5,2,1,3:T(8,128)(2,1)S(1)} %slice.27, bf16[64,4,4,1,8,17]{0,4,5,2,1,3:T(8,128)(2,1)S(1)} %copy.85, pred[8,17]{0,1:T(8,128)(4,1)S(1)} %copy-done.5, bf16[64,64]{0,1:T(8,128)(2,1)S(1)} %compare_convert_fusion, bf16[64,8,3,3,3]{0,1,4,3,2:T(8,128)(2,1)S(1)} %constant_dynamic-slice_fusion), kind=kOutput, calls=%fused_computation.8 | convolution fusion | flops 202055680 | bytes 482440 | tf_op jit(solution)/shard_map/conv_general_dilated | solution.py:30
  66.9 0.2 copy.86
  67.1 0.2 slice_bitcast_fusion
  67.3 0.8 copy.87
  68.1 3.3 %all-to-all-start.3 = ((bf16[64,4,2,128]{3,0,2,1:T(8,128)(2,1)}), bf16[64,4,2,128]{3,0,2,1:T(8,128)(2,1)S(1)}, u32[]{:S(2)}, u32[]{:S(2)}) async-start(bf16[64,4,2,128]{3,0,2,1:T(8,128)(2,1)} %copy.87), calls=%async_computation.3 | async-start | bytes 262144 | tf_op jit(solution)/shard_map/all_to_all | solution.py:114
  71.4 0.2 all-reduce.4.cloned.1.call-start
  71.7 7.9 %fusion.3 = f32[8,64,3,3,3]{1,0,4,3,2:T(8,128)S(1)} fusion(bf16[1,64,6,4,130]{1,0,4,3,2:T(2,128)(2,1)S(1)} %copy.93, bf16[1,64,4,2,128]{1,0,4,3,2:T(2,128)(2,1)S(1)} %copy.94, f32[8,64]{1,0:T(8,128)S(1)} %fusion.40), kind=kOutput, calls=%fused_computation.7 | convolution fusion | flops 226699776 | bytes 587776 | tf_op jit(solution)/shard_map/conv_general_dilated | solution.py:59
  79.6 11.5 %psum.22 = f32[64,8,3,3,3]{0,1,4,3,2:T(8,128)S(1)} all-reduce(f32[64,8,3,3,3]{0,1,4,3,2:T(8,128)S(1)} %bitcast.154), channel_id=1, replica_groups=mesh['rep'=2,'grp'=4,'sub'=4] {'sub'}, use_global_device_ids=true, to_apply=%region_2.3 | all-reduce | flops 13824 | bytes 110592 | tf_op jit(solution)/shard_map/psum | solution.py:115
  91.2 0.2 copy.101
  91.4 0.3 reshape.178
  91.8 0.1 multiply_convert_fusion
  91.9 0.9 convolution_bitcast_fusion.1
  92.8 0.0 all-reduce.4.cloned.1.call-update
  92.9 0.7 broadcast_multiply_fusion.2
  93.5 0.2 fusion.7
  93.7 0.8 copy.97
  94.5 89.9 %all-reduce.4.cloned.1.call-done = (f32[256,256]{0,1:T(8,128)}, f32[256,256]{0,1:T(8,128)}) async-done(((f32[256,256]{0,1:T(8,128)}, f32[256,256]{0,1:T(8,128)}), (f32[256,256]{0,1:T(8,128)}, f32[256,256]{0,1:T(8,128)})) %all-reduce.4.cloned.1.call-update) | async-done | bytes 524304 | tf_op jit(solution)/shard_map/psum | solution.py:130
  184.5 1.1 broadcast_multiply_fusion
  185.5 0.8 copy.98
  186.4 0.8 copy.99
  (25 shorter events, 0.3 us)
Async XLA Ops:
  7.2 36.6 %copy-start = (bf16[256,256]{1,0:T(8,128)(2,1)S(1)}, bf16[256,256]{1,0:T(8,128)(2,1)}, u32[]{:S(2)}) copy-start(bf16[256,256]{1,0:T(8,128)(2,1)} %param.9) | copy-start | bytes 393220
  8.2 20.1 %copy-start.4 = (bf16[256,8,3,3,3]{0,1,4,3,2:T(8,128)(2,1)S(1)}, bf16[256,8,3,3,3]{0,1,4,3,2:T(8,128)(2,1)}, u32[]{:S(2)}) copy-start(bf16[256,8,3,3,3]{0,1,4,3,2:T(8,128)(2,1)} %param.8) | copy-start | bytes 331780
  10.9 10.2 %all-to-all-start = ((bf16[256,1,2,128]{3,2,1,0:T(2,128)(2,1)}), bf16[256,1,2,128]{3,2,1,0:T(2,128)(2,1)S(1)}, u32[]{:S(2)}, u32[]{:S(2)}) async-start(bf16[256,1,2,128]{3,2,1,0:T(2,128)(2,1)} %copy.71), calls=%async_computation | async-start | bytes 262144 | tf_op jit(solution)/shard_map/all_to_all | solution.py:85
  21.1 7.3 %collective-permute-start = (bf16[64,4,1,128]{3,0,1,2:T(8,128)(2,1)S(1)}, bf16[64,4,1,128]{3,0,1,2:T(8,128)(2,1)S(1)}, u32[]{:S(2)}, u32[]{:S(2)}) collective-permute-start(bf16[64,4,1,128]{3,0,1,2:T(8,128)(2,1)S(1)} %get-tuple-element.33), channel_id=1, source_target_pairs={{0,1},{1,2},{2,3},{4,5},{5,6},{6,7},{8,9},{9,10},{10,11},{12,13},{... | collective-permute-start | bytes 196616 | tf_op jit(solution)/shard_map/ppermute | solution.py:15
  26.4 5.6 %collective-permute-start.1 = (bf16[64,4,1,128]{3,0,1,2:T(8,128)(2,1)S(1)}, bf16[64,4,1,128]{3,0,1,2:T(8,128)(2,1)S(1)}, u32[]{:S(2)}, u32[]{:S(2)}) collective-permute-start(bf16[64,4,1,128]{3,0,1,2:T(8,128)(2,1)S(1)} %get-tuple-element.34), channel_id=1, source_target_pairs={{1,0},{2,1},{3,2},{5,4},{6,5},{7,6},{9,8},{10,9},{11,10},{13,12},{... | collective-permute-start | bytes 196616 | tf_op jit(solution)/shard_map/ppermute | solution.py:18
  32.3 0.7 copy-start.5
  34.5 4.3 %copy-start.2 = (bf16[256,1,2,128]{3,2,1,0:T(2,128)(2,1)S(1)}, bf16[256,1,2,128]{3,2,1,0:T(2,128)(2,1)}, u32[]{:S(2)}) copy-start(bf16[256,1,2,128]{3,2,1,0:T(2,128)(2,1)} %param.6) | copy-start | bytes 393220
  35.5 8.1 %all-to-all-start.1 = ((bf16[64,4,2,128]{3,0,2,1:T(8,128)(2,1)}), bf16[64,4,2,128]{3,0,2,1:T(8,128)(2,1)S(1)}, u32[]{:S(2)}, u32[]{:S(2)}) async-start(bf16[64,4,2,128]{3,0,2,1:T(8,128)(2,1)} %fusion.28), calls=%async_computation.1 | async-start | bytes 262144 | tf_op jit(solution)/shard_map/all_to_all | solution.py:89
  46.0 8.6 %all-to-all-start.2 = ((bf16[256,1,2,128]{3,2,1,0:T(2,128)(2,1)}), bf16[256,1,2,128]{3,2,1,0:T(2,128)(2,1)S(1)}, u32[]{:S(2)}, u32[]{:S(2)}) async-start(bf16[256,1,2,128]{3,2,1,0:T(2,128)(2,1)} %copy.80), calls=%async_computation.2 | async-start | bytes 262144 | tf_op jit(solution)/shard_map/all_to_all | solution.py:107
  54.8 6.0 %collective-permute-start.2 = (bf16[64,4,1,128]{3,0,2,1:T(8,128)(2,1)S(1)}, bf16[64,4,1,128]{3,0,2,1:T(8,128)(2,1)S(1)}, u32[]{:S(2)}, u32[]{:S(2)}) collective-permute-start(bf16[64,4,1,128]{3,0,2,1:T(8,128)(2,1)S(1)} %get-tuple-element.31), channel_id=1, source_target_pairs={{0,1},{1,2},{2,3},{4,5},{5,6},{6,7},{8,9},{9,10},{10,11},{12,13},{... | collective-permute-start | bytes 196616 | tf_op jit(solution)/shard_map/ppermute | solution.py:15
  58.4 5.6 %collective-permute-start.3 = (bf16[64,4,1,128]{3,0,2,1:T(8,128)(2,1)S(1)}, bf16[64,4,1,128]{3,0,2,1:T(8,128)(2,1)S(1)}, u32[]{:S(2)}, u32[]{:S(2)}) collective-permute-start(bf16[64,4,1,128]{3,0,2,1:T(8,128)(2,1)S(1)} %get-tuple-element.32), channel_id=1, source_target_pairs={{1,0},{2,1},{3,2},{5,4},{6,5},{7,6},{9,8},{10,9},{11,10},{13,12},{... | collective-permute-start | bytes 196616 | tf_op jit(solution)/shard_map/ppermute | solution.py:18
  68.1 23.1 %all-to-all-start.3 = ((bf16[64,4,2,128]{3,0,2,1:T(8,128)(2,1)}), bf16[64,4,2,128]{3,0,2,1:T(8,128)(2,1)S(1)}, u32[]{:S(2)}, u32[]{:S(2)}) async-start(bf16[64,4,2,128]{3,0,2,1:T(8,128)(2,1)} %copy.87), calls=%async_computation.3 | async-start | bytes 262144 | tf_op jit(solution)/shard_map/all_to_all | solution.py:114
  71.4 113.0 %all-reduce.4.cloned.1.call-start = ((), (), s32[]{:S(2)}) async-start(), calls=%async_computation.4 | async-start | bytes 1048576 | tf_op jit(solution)/shard_map/psum | solution.py:130
  79.6 12.2 %copy-start.1 = (f32[256,256]{0,1:T(8,128)S(1)}, f32[256,256]{0,1:T(8,128)}, u32[]{:S(2)}) copy-start(f32[256,256]{0,1:T(8,128)} %get-tuple-element.36) | copy-start | bytes 786436
  91.4 2.1 %copy-start.3 = (bf16[256,256]{1,0:T(8,128)(2,1)S(1)}, bf16[256,256]{1,0:T(8,128)(2,1)}, u32[]{:S(2)}) copy-start(bf16[256,256]{1,0:T(8,128)(2,1)} %param.7) | copy-start | bytes 393220
Sparse Core Ops, SparseCore 0:
  93.0 91.4 all-reduce.3
where the time goes:
time: 195 us; the launch traced here: 194 us
  waiting for transfers between devices  106 us (54%)
  starting transfers between devices  28.3 us (15%)
  matrix products  16.7 us (9%)
  between operations  14.5 us (7%)
  local copies, waits for them, and re-layouts  13.7 us (7%)
  blocking collectives  11.5 us (6%)
  other arithmetic  2.91 us (1%)
    psum x1, waiting for transfers between devices, per_device(): first_grad = lax.psum(first_part, ('grp', 'sub')) * factor  89.9 us
    psum x1, blocking collectives, per_device(): group_grad = lax.psum(kernel_part, 'sub') * factor  11.5 us
    ppermute x2, starting transfers between devices, padded_2(): lax.ppermute(lax.slice_in_dim(block, block.shape[dim] - width, None, axis...  8.89 us
    conv_general_dilated x1, matrix products, weight_grad(): lax.conv_general_dilated(padded[None], deltas[None], (1, 1, 1), 'VALID',...  7.92 us
    ppermute x2, waiting for transfers between devices, padded_2(): lax.ppermute(lax.slice_in_dim(block, 0, width, axis=dim), axis, backward)  6.74 us
    unnamed x21, local copies, waits for them, and re-layouts  5.57 us
    all_to_all x1, starting transfers between devices, per_device(): lax.all_to_all(first_act, 'grp', split_axis=0, concat_axis=1, tiled=True)  5.42 us
    all_to_all x1, waiting for transfers between devices, per_device(): lax.all_to_all(first_act, 'grp', split_axis=0, concat_axis=1, tiled=True)  4.73 us
  transfers between devices with their start and end apart: 9, of which 6 were waited for; matrix products, arithmetic and copies ran while one was open for 8% of the time, Pallas kernels for 0%

commit v1 on v0

--- a/solution.py
+++ b/solution.py
@@ -127,7 +127,12 @@
         .astype(jnp.bfloat16)
         .reshape(volume.shape)
     )
-    first_grad = lax.psum(first_part, ("grp", "sub")) * factor
+
+    def lay_the_sector(field_in, shard_axis, group_axis):
+        step_out = lax.psum(field_in, shard_axis)
+        return lax.psum(step_out, group_axis)
+
+    first_grad = lay_the_sector(first_part, "sub", "grp") * factor
     return (block_output, volume_grad, first_grad, group_grad, third_grad)
 
 

time: 195 us -> 242 us (1.24)
  waiting for transfers between devices: 106 us -> 146 us
    psum x1 -> x3, waiting for transfers between devices: 89.9 us -> 129 us  [the longest x1 84.1 us: per_device(): third_grad = lax.psum(third_part, ('grp', 'sub')) * factor]
    all_to_all x1, waiting for transfers between devices: 0.01 us -> 4.24 us  [per_device(): lax.all_to_all(inner_local, 'grp', split_axis=1, concat_axis=0, tiled=True)]
    ppermute x2, waiting for transfers between devices: 6.74 us -> 3.54 us  [padded_2(): lax.ppermute(lax.slice_in_dim(block, 0, width, axis=dim), axis, backward)]
    unnamed x21 -> x19, local copies, waits for them, and re-layouts: 5.57 us -> 5.56 us
  transfers between devices with their start and end apart: 9 -> 11, of which waited for: 6 -> 8; matrix products, arithmetic and copies ran while one was open for 8% -> 7% of each run, Pallas kernels for 0% -> 0%
where the time goes in v1:
time: 242 us; the launch traced here: 239 us
  waiting for transfers between devices  146 us (60%)
  starting transfers between devices  28.4 us (12%)
  matrix products  16.7 us (7%)
  between operations  15.9 us (7%)
  local copies, waits for them, and re-layouts  13.7 us (6%)
  blocking collectives  13.3 us (5%)
  other arithmetic  4.72 us (2%)
    psum x1, waiting for transfers between devices, per_device(): third_grad = lax.psum(third_part, ('grp', 'sub')) * factor  84.1 us
    psum x1, waiting for transfers between devices, lay_the_sector(): return lax.psum(step_out, group_axis)  35.3 us
    psum x1, blocking collectives, per_device(): group_grad = lax.psum(kernel_part, 'sub') * factor  13.3 us
    psum x1, waiting for transfers between devices, lay_the_sector(): step_out = lax.psum(field_in, shard_axis)  9.17 us
    ppermute x2, starting transfers between devices, padded_2(): lax.ppermute(lax.slice_in_dim(block, block.shape[dim] - width, None, axis...  8.89 us
    conv_general_dilated x1, matrix products, weight_grad(): lax.conv_general_dilated(padded[None], deltas[None], (1, 1, 1), 'VALID',...  7.94 us
    unnamed x19, local copies, waits for them, and re-layouts  5.56 us
    all_to_all x1, starting transfers between devices, per_device(): lax.all_to_all(first_act, 'grp', split_axis=0, concat_axis=1, tiled=True)  5.42 us
  transfers between devices with their start and end apart: 11, of which 8 were waited for; matrix products, arithmetic and copies ran while one was open for 7% of the time, Pallas kernels for 0%

profile of v1, /device:TPU:1, one launch (start us, length us, event | category | flops | bytes accessed | tf_op | source)
XLA Modules:
  0.0 238.8 jit_solution(15135224706127462871)
XLA Ops:
  8.0 1.0 copy.70
  9.1 1.8 multiply_convert_fusion.2
  10.9 0.8 copy.71
  11.7 5.4 %all-to-all-start = ((bf16[256,1,2,128]{3,2,1,0:T(2,128)(2,1)}), bf16[256,1,2,128]{3,2,1,0:T(2,128)(2,1)S(1)}, u32[]{:S(2)}, u32[]{:S(2)}) async-start(bf16[256,1,2,128]{3,2,1,0:T(2,128)(2,1)} %copy.71), calls=%async_computation | async-start | bytes 262144 | tf_op jit(solution)/shard_map/all_to_all | solution.py:85
  17.1 0.1 compare_convert_fusion
  17.2 4.7 %all-to-all-done = bf16[256,1,2,128]{3,2,1,0:T(2,128)(2,1)S(1)} async-done(((bf16[256,1,2,128]{3,2,1,0:T(2,128)(2,1)}), bf16[256,1,2,128]{3,2,1,0:T(2,128)(2,1)S(1)}, u32[]{:S(2)}, u32[]{:S(2)}) %all-to-all-start) | async-done | bytes 131104 | tf_op jit(solution)/shard_map/all_to_all | solution.py:85
  22.0 5.2 %collective-permute-start = (bf16[64,4,1,128]{3,0,1,2:T(8,128)(2,1)S(1)}, bf16[64,4,1,128]{3,0,1,2:T(8,128)(2,1)S(1)}, u32[]{:S(2)}, u32[]{:S(2)}) collective-permute-start(bf16[64,4,1,128]{3,0,1,2:T(8,128)(2,1)S(1)} %get-tuple-element.31), channel_id=1, source_target_pairs={{0,1},{1,2},{2,3},{4,5},{5,6},{6,7},{8,9},{9,10},{10,11},{12,13},{... | collective-permute-start | bytes 196616 | tf_op jit(solution)/shard_map/ppermute | solution.py:15
  27.2 1.9 collective-permute-start.1
  29.1 0.1 constant_dynamic-slice_fusion
  29.2 3.5 %collective-permute-done.1 = bf16[64,4,1,128]{3,0,1,2:T(8,128)(2,1)S(1)} collective-permute-done((bf16[64,4,1,128]{3,0,1,2:T(8,128)(2,1)S(1)}, bf16[64,4,1,128]{3,0,1,2:T(8,128)(2,1)S(1)}, u32[]{:S(2)}, u32[]{:S(2)}) %collective-permute-start.1) | collective-permute-done | bytes 65568 | tf_op jit(solution)/shard_map/ppermute | solution.py:18
  32.8 0.3 copy.107
  33.2 0.3 pad.5.clone
  33.4 0.1 copy.75
  33.6 0.3 copy-done.4
  33.8 1.2 add_multiply_fusion
  35.1 0.3 copy.76
  35.4 0.2 copy.105
  35.6 0.7 fusion.28
  36.4 3.3 %all-to-all-start.1 = ((bf16[64,4,2,128]{3,0,2,1:T(8,128)(2,1)}), bf16[64,4,2,128]{3,0,2,1:T(8,128)(2,1)S(1)}, u32[]{:S(2)}, u32[]{:S(2)}) async-start(bf16[64,4,2,128]{3,0,2,1:T(8,128)(2,1)} %fusion.28), calls=%async_computation.1 | async-start | bytes 262144 | tf_op jit(solution)/shard_map/all_to_all | solution.py:89
  39.7 0.8 copy.79
  40.5 0.3 copy.91
  40.9 0.2 copy.106
  41.0 0.2 pad_bitcast_fusion
  41.3 1.7 copy.93
  43.0 1.4 all-to-all-done.1
  44.4 0.1 copy.78
  44.6 1.3 fusion.24
  45.9 0.2 convolution_convert_fusion
  46.1 0.8 copy.80
  46.9 3.3 %all-to-all-start.2 = ((bf16[256,1,2,128]{3,2,1,0:T(2,128)(2,1)}), bf16[256,1,2,128]{3,2,1,0:T(2,128)(2,1)S(1)}, u32[]{:S(2)}, u32[]{:S(2)}) async-start(bf16[256,1,2,128]{3,2,1,0:T(2,128)(2,1)} %copy.80), calls=%async_computation.2 | async-start | bytes 262144 | tf_op jit(solution)/shard_map/all_to_all | solution.py:107
  50.2 0.9 fusion.35
  51.2 0.8 copy.96
  52.0 3.5 %all-to-all-done.2 = bf16[256,1,2,128]{3,2,1,0:T(2,128)(2,1)S(1)} async-done(((bf16[256,1,2,128]{3,2,1,0:T(2,128)(2,1)}), bf16[256,1,2,128]{3,2,1,0:T(2,128)(2,1)S(1)}, u32[]{:S(2)}, u32[]{:S(2)}) %all-to-all-start.2) | async-done | bytes 131104 | tf_op jit(solution)/shard_map/all_to_all | solution.py:107
  55.5 0.1 fusion.23
  55.6 3.7 %collective-permute-start.2 = (bf16[64,4,1,128]{3,0,2,1:T(8,128)(2,1)S(1)}, bf16[64,4,1,128]{3,0,2,1:T(8,128)(2,1)S(1)}, u32[]{:S(2)}, u32[]{:S(2)}) collective-permute-start(bf16[64,4,1,128]{3,0,2,1:T(8,128)(2,1)S(1)} %get-tuple-element.29), channel_id=1, source_target_pairs={{0,1},{1,2},{2,3},{4,5},{5,6},{6,7},{8,9},{9,10},{10,11},{12,13},{... | collective-permute-start | bytes 196616 | tf_op jit(solution)/shard_map/ppermute | solution.py:15
  59.3 1.9 collective-permute-start.3
  61.2 84.1 %all-reduce.9.cloned.1.call-done = f32[256,256]{0,1:T(8,128)} async-done(((f32[256,256]{0,1:T(8,128)}), f32[256,256]{0,1:T(8,128)}) %all-reduce.9.cloned.1.call-update) | async-done | bytes 262160 | tf_op jit(solution)/shard_map/psum | solution.py:101
  145.3 1.0 broadcast_multiply_fusion
  146.3 0.8 copy.99
  147.2 0.3 copy.108
  147.5 0.3 pad.7.clone
  147.8 0.1 copy.85
  147.9 2.1 fusion.4
  150.0 0.2 copy.86
  150.2 0.2 slice_bitcast_fusion
  150.4 0.8 copy.87
  151.2 3.3 %all-to-all-start.3 = ((bf16[64,4,2,128]{3,0,2,1:T(8,128)(2,1)}), bf16[64,4,2,128]{3,0,2,1:T(8,128)(2,1)S(1)}, u32[]{:S(2)}, u32[]{:S(2)}) async-start(bf16[64,4,2,128]{3,0,2,1:T(8,128)(2,1)} %copy.87), calls=%async_computation.3 | async-start | bytes 262144 | tf_op jit(solution)/shard_map/all_to_all | solution.py:114
  154.5 0.0 all-reduce.5.cloned.1.call-start
  154.6 0.4 copy.94
  155.0 4.2 %all-to-all-done.3 = bf16[64,4,2,128]{3,0,2,1:T(8,128)(2,1)S(1)} async-done(((bf16[64,4,2,128]{3,0,2,1:T(8,128)(2,1)}), bf16[64,4,2,128]{3,0,2,1:T(8,128)(2,1)S(1)}, u32[]{:S(2)}, u32[]{:S(2)}) %all-to-all-start.3) | async-done | bytes 131104 | tf_op jit(solution)/shard_map/all_to_all | solution.py:114
  159.3 0.2 copy.101
  159.5 0.3 reshape.178
  159.8 1.1 multiply_convert_fusion
  160.9 0.9 convolution_bitcast_fusion.1
  161.9 0.2 all-reduce.7.cloned.1.call-start
  162.1 7.9 %fusion.3 = f32[8,64,3,3,3]{1,0,4,3,2:T(8,128)S(1)} fusion(bf16[1,64,6,4,130]{1,0,4,3,2:T(2,128)(2,1)S(1)} %copy.93, bf16[1,64,4,2,128]{1,0,4,3,2:T(2,128)(2,1)S(1)} %copy.94, f32[8,64]{1,0:T(8,128)S(1)} %fusion.40), kind=kOutput, calls=%fused_computation.7 | convolution fusion | flops 226699776 | bytes 587776 | tf_op jit(solution)/shard_map/conv_general_dilated | solution.py:59
  170.1 13.3 %psum.30 = f32[64,8,3,3,3]{0,1,4,3,2:T(8,128)S(1)} all-reduce(f32[64,8,3,3,3]{0,1,4,3,2:T(8,128)S(1)} %bitcast.154), channel_id=1, replica_groups=mesh['rep'=2,'grp'=4,'sub'=4] {'sub'}, use_global_device_ids=true, to_apply=%region_3.4 | all-reduce | flops 13824 | bytes 110592 | tf_op jit(solution)/shard_map/psum | solution.py:115
  183.3 9.2 %all-reduce.5.cloned.1.call-done = f32[256,256]{0,1:T(8,128)} async-done(((f32[256,256]{0,1:T(8,128)}), f32[256,256]{0,1:T(8,128)}) %all-reduce.5.cloned.1.call-update) | async-done | bytes 262160 | tf_op jit(solution)/shard_map/psum | solution.py:132
  192.5 0.7 broadcast_multiply_fusion.2
  193.2 0.2 fusion.7
  193.4 0.8 copy.97
  194.2 35.3 %all-reduce.7.cloned.1.call-done = f32[256,256]{0,1:T(8,128)} async-done(((f32[256,256]{0,1:T(8,128)}), f32[256,256]{0,1:T(8,128)}) %all-reduce.7.cloned.1.call-update) | async-done | bytes 262160 | tf_op jit(solution)/shard_map/psum | solution.py:133
  229.5 1.0 broadcast_multiply_fusion.1
  230.5 0.8 copy.98
  (30 shorter events, 0.4 us)
Async XLA Ops:
  8.0 36.6 %copy-start = (bf16[256,256]{1,0:T(8,128)(2,1)S(1)}, bf16[256,256]{1,0:T(8,128)(2,1)}, u32[]{:S(2)}) copy-start(bf16[256,256]{1,0:T(8,128)(2,1)} %param.9) | copy-start | bytes 393220
  9.1 20.1 %copy-start.3 = (bf16[256,8,3,3,3]{0,1,4,3,2:T(8,128)(2,1)S(1)}, bf16[256,8,3,3,3]{0,1,4,3,2:T(8,128)(2,1)}, u32[]{:S(2)}) copy-start(bf16[256,8,3,3,3]{0,1,4,3,2:T(8,128)(2,1)} %param.8) | copy-start | bytes 331780
  11.7 10.2 %all-to-all-start = ((bf16[256,1,2,128]{3,2,1,0:T(2,128)(2,1)}), bf16[256,1,2,128]{3,2,1,0:T(2,128)(2,1)S(1)}, u32[]{:S(2)}, u32[]{:S(2)}) async-start(bf16[256,1,2,128]{3,2,1,0:T(2,128)(2,1)} %copy.71), calls=%async_computation | async-start | bytes 262144 | tf_op jit(solution)/shard_map/all_to_all | solution.py:85
  22.0 7.3 %collective-permute-start = (bf16[64,4,1,128]{3,0,1,2:T(8,128)(2,1)S(1)}, bf16[64,4,1,128]{3,0,1,2:T(8,128)(2,1)S(1)}, u32[]{:S(2)}, u32[]{:S(2)}) collective-permute-start(bf16[64,4,1,128]{3,0,1,2:T(8,128)(2,1)S(1)} %get-tuple-element.31), channel_id=1, source_target_pairs={{0,1},{1,2},{2,3},{4,5},{5,6},{6,7},{8,9},{9,10},{10,11},{12,13},{... | collective-permute-start | bytes 196616 | tf_op jit(solution)/shard_map/ppermute | solution.py:15
  27.2 5.6 %collective-permute-start.1 = (bf16[64,4,1,128]{3,0,1,2:T(8,128)(2,1)S(1)}, bf16[64,4,1,128]{3,0,1,2:T(8,128)(2,1)S(1)}, u32[]{:S(2)}, u32[]{:S(2)}) collective-permute-start(bf16[64,4,1,128]{3,0,1,2:T(8,128)(2,1)S(1)} %get-tuple-element.32), channel_id=1, source_target_pairs={{1,0},{2,1},{3,2},{5,4},{6,5},{7,6},{9,8},{10,9},{11,10},{13,12},{... | collective-permute-start | bytes 196616 | tf_op jit(solution)/shard_map/ppermute | solution.py:18
  33.1 0.7 copy-start.4
  35.4 4.3 %copy-start.1 = (bf16[256,1,2,128]{3,2,1,0:T(2,128)(2,1)S(1)}, bf16[256,1,2,128]{3,2,1,0:T(2,128)(2,1)}, u32[]{:S(2)}) copy-start(bf16[256,1,2,128]{3,2,1,0:T(2,128)(2,1)} %param.6) | copy-start | bytes 393220
  36.4 8.1 %all-to-all-start.1 = ((bf16[64,4,2,128]{3,0,2,1:T(8,128)(2,1)}), bf16[64,4,2,128]{3,0,2,1:T(8,128)(2,1)S(1)}, u32[]{:S(2)}, u32[]{:S(2)}) async-start(bf16[64,4,2,128]{3,0,2,1:T(8,128)(2,1)} %fusion.28), calls=%async_computation.1 | async-start | bytes 262144 | tf_op jit(solution)/shard_map/all_to_all | solution.py:89
  46.9 8.6 %all-to-all-start.2 = ((bf16[256,1,2,128]{3,2,1,0:T(2,128)(2,1)}), bf16[256,1,2,128]{3,2,1,0:T(2,128)(2,1)S(1)}, u32[]{:S(2)}, u32[]{:S(2)}) async-start(bf16[256,1,2,128]{3,2,1,0:T(2,128)(2,1)} %copy.80), calls=%async_computation.2 | async-start | bytes 262144 | tf_op jit(solution)/shard_map/all_to_all | solution.py:107
  50.2 95.1 %all-reduce.9.cloned.1.call-start = ((), (), s32[]{:S(2)}) async-start(), calls=%async_computation.6 | async-start | bytes 524288 | tf_op jit(solution)/shard_map/psum | solution.py:101
  55.6 91.5 %collective-permute-start.2 = (bf16[64,4,1,128]{3,0,2,1:T(8,128)(2,1)S(1)}, bf16[64,4,1,128]{3,0,2,1:T(8,128)(2,1)S(1)}, u32[]{:S(2)}, u32[]{:S(2)}) collective-permute-start(bf16[64,4,1,128]{3,0,2,1:T(8,128)(2,1)S(1)} %get-tuple-element.29), channel_id=1, source_target_pairs={{0,1},{1,2},{2,3},{4,5},{5,6},{6,7},{8,9},{9,10},{10,11},{12,13},{... | collective-permute-start | bytes 196616 | tf_op jit(solution)/shard_map/ppermute | solution.py:15
  59.3 87.8 %collective-permute-start.3 = (bf16[64,4,1,128]{3,0,2,1:T(8,128)(2,1)S(1)}, bf16[64,4,1,128]{3,0,2,1:T(8,128)(2,1)S(1)}, u32[]{:S(2)}, u32[]{:S(2)}) collective-permute-start(bf16[64,4,1,128]{3,0,2,1:T(8,128)(2,1)S(1)} %get-tuple-element.30), channel_id=1, source_target_pairs={{1,0},{2,1},{3,2},{5,4},{6,5},{7,6},{9,8},{10,9},{11,10},{13,12},{... | collective-permute-start | bytes 196616 | tf_op jit(solution)/shard_map/ppermute | solution.py:18
  151.2 8.1 %all-to-all-start.3 = ((bf16[64,4,2,128]{3,0,2,1:T(8,128)(2,1)}), bf16[64,4,2,128]{3,0,2,1:T(8,128)(2,1)S(1)}, u32[]{:S(2)}, u32[]{:S(2)}) async-start(bf16[64,4,2,128]{3,0,2,1:T(8,128)(2,1)} %copy.87), calls=%async_computation.3 | async-start | bytes 262144 | tf_op jit(solution)/shard_map/all_to_all | solution.py:114
  154.5 38.0 %all-reduce.5.cloned.1.call-start = ((), (), s32[]{:S(2)}) async-start(), calls=%async_computation.4 | async-start | bytes 524288 | tf_op jit(solution)/shard_map/psum | solution.py:132
  161.9 31.3 %copy-start.2 = (bf16[256,256]{1,0:T(8,128)(2,1)S(1)}, bf16[256,256]{1,0:T(8,128)(2,1)}, u32[]{:S(2)}) copy-start(bf16[256,256]{1,0:T(8,128)(2,1)} %param.7) | copy-start | bytes 393220
  161.9 67.6 %all-reduce.7.cloned.1.call-start = ((), (), s32[]{:S(2)}) async-start(), calls=%async_computation.5 | async-start | bytes 524288 | tf_op jit(solution)/shard_map/psum | solution.py:133
Sparse Core Ops, SparseCore 0:
  55.0 90.2 all-reduce.8
Sparse Core Ops, SparseCore 1:
  161.9 30.5 all-reduce.4
  194.8 34.7 all-reduce.6
